TPU v7x, 256 devices: a whole 4x4x8 slice. The times are simulated.
256 devices in a mesh: dp: 8 (over z), expert: 32 (over y, x, core).
Axes of the slice: x: 4, y: 4, z: 8, core: 2. Of those that a mesh axis runs over, the one named last changes fastest.
Arguments:
- tokens: bfloat16 [32, 16, 7168], P('expert', 'dp'), may hold values from -6 to 6
- tangent: bfloat16 [32, 16, 7168], P('expert', 'dp'), may hold values from -52 to 52
- route_ids: int32 [32, 16, 8], P('expert', 'dp'), may hold values from 0 to 31, all different within a row; in each aligned block of 16 rows (0 to 15, 16 to 31, ..., all dimensions but the last counted through in order) at most 8 rows name the same one
- gate_fixed: int32 [32, 16, 8], P('expert', 'dp'), may hold values from 4096 to 65535
- gate_proj: bfloat16 [32, 7168, 2048], P('expert', None, 'dp'), may hold values from -0.0625 to 0.0625
- up_proj: bfloat16 [32, 7168, 2048], P('expert', None, 'dp'), may hold values from -0.0625 to 0.0625
- down_proj: bfloat16 [32, 2048, 7168], P('expert', 'dp'), may hold values from -0.125 to 0.125
Outputs:
- next_tangent: bfloat16 [32, 16, 7168], P('expert', 'dp')
- lipschitz: float32 [], replicated
Inputs may be any that keep to these rules, and one draw needn't show every extreme that they name: `route_ids`: each token names 8 different experts; within one group of 16 tokens no expert is named by more than 8 tokens.
All inputs are finite; a program needn't handle non-finite values.
Results may differ from a plain program's by a relative error of at most 0.0065.
Values may be sent and summed in bfloat16 or wider, within the bound.
No kernel may reach another device: no remote copies, remote signals or barrier semaphores. Data moves between devices by JAX's collectives and lax.ppermute only.
A program may use at most 128 MiB of HBM per device.

v0:
```python
import jax
import jax.numpy as jnp
from jax import lax
from jax.sharding import PartitionSpec as P

BF16 = jnp.bfloat16
F32 = jnp.float32


def silu_parts(gate_pre):
    sigmoid_val = jax.nn.sigmoid(gate_pre)
    return (gate_pre * sigmoid_val, sigmoid_val * (1.0 + gate_pre * (1.0 - sigmoid_val)))


def contract_last(left, right):
    return lax.dot_general(left, right, (((1,), (1,)), ((), ())), preferred_element_type=F32)


def exchange(value):
    return lax.all_to_all(value, "expert", split_axis=0, concat_axis=0, tiled=True)


def body(tokens, tangent, route_ids, gate_fixed, gate_proj, up_proj, down_proj):
    model_width = tokens.shape[2]
    tok_dev = tokens.shape[1]
    top_count = route_ids.shape[2]
    experts = lax.axis_size("expert")
    gates_local = gate_fixed[0]
    pieces = [
        tokens[0],
        tangent[0],
        route_ids[0].astype(BF16),
        (gates_local // 256).astype(BF16),
        (gates_local % 256).astype(BF16),
    ]
    width = 2 * model_width + 3 * top_count
    pad = -width % 128
    if pad:
        pieces.append(jnp.zeros((tok_dev, pad), BF16))
    packed = jnp.concatenate(pieces, axis=1)
    col = lax.all_gather(packed, "dp", axis=0, tiled=True)
    col_count = col.shape[0]
    meta = col[:, 2 * model_width : width].astype(jnp.int32)
    col_ids = meta[:, :top_count]
    col_gates = meta[:, top_count : 2 * top_count] * 256 + meta[:, 2 * top_count :]
    col_pair = jnp.concatenate(
        [col[:, :model_width], col[:, model_width : 2 * model_width]], axis=0
    )
    capacity = min(col_count, 2 * col_count * top_count // experts)
    slot_total = experts * capacity
    flat_ids = col_ids.reshape(-1)
    experts_all = jnp.arange(experts, dtype=jnp.int32)
    onehot = (flat_ids[:, None] == experts_all[None, :]).astype(jnp.int32)
    earlier = jnp.cumsum(onehot, axis=0) - onehot
    slot_place = jnp.sum(earlier * onehot, axis=1)
    target = flat_ids * capacity + slot_place
    places = jnp.arange(slot_total, dtype=jnp.int32)
    matches = target[:, None] == places[None, :]
    route_f = jnp.sum(matches.reshape(col_count, top_count, slot_total), axis=1).astype(F32).T
    route_map = route_f.astype(BF16)
    gate_vals = col_gates.reshape(-1).astype(F32) / 65536.0
    combine_map = jnp.sum(
        jnp.where(matches, gate_vals[:, None], 0.0).reshape(col_count, top_count, slot_total),
        axis=1,
    )
    eye2 = jnp.eye(2, dtype=F32)
    pair_map = (
        (route_f.reshape(experts, 1, capacity, 1, col_count) * eye2.reshape(1, 2, 1, 2, 1))
        .reshape(experts * 2 * capacity, 2 * col_count)
        .astype(BF16)
    )
    send_pair = (
        jnp.dot(pair_map, col_pair, preferred_element_type=F32)
        .astype(BF16)
        .reshape(experts, 2 * capacity, model_width)
    )
    weight_gate = gate_proj[0]
    weight_up = up_proj[0]
    weight_down = down_proj[0]
    hidden_dev = weight_gate.shape[1]
    rows_pair = exchange(send_pair)
    groups_here = rows_pair.shape[0]
    flat_pair = rows_pair.reshape(-1, model_width)
    gate_both = jnp.dot(flat_pair, weight_gate, preferred_element_type=F32).reshape(
        groups_here, 2, capacity, hidden_dev
    )
    up_both = jnp.dot(flat_pair, weight_up, preferred_element_type=F32).reshape(
        groups_here, 2, capacity, hidden_dev
    )
    gate_pre = gate_both[:, 0].reshape(-1, hidden_dev)
    gate_dir = gate_both[:, 1].reshape(-1, hidden_dev)
    up_pre = up_both[:, 0].reshape(-1, hidden_dev)
    up_dir = up_both[:, 1].reshape(-1, hidden_dev)
    silu_value, silu_slope = silu_parts(gate_pre)
    jvp_hidden = (silu_slope * gate_dir * up_pre + silu_value * up_dir).astype(BF16)
    partial_value = jnp.dot(jvp_hidden, weight_down, preferred_element_type=F32)
    returned = exchange(partial_value.astype(BF16).reshape(groups_here, capacity, model_width))
    gate_coef = silu_slope * up_pre
    up_coef = silu_value
    product_part = jnp.dot(
        combine_map,
        returned.reshape(slot_total, -1).astype(F32),
        precision=lax.Precision.HIGHEST,
        preferred_element_type=F32,
    )
    product_bf = lax.psum(product_part, "dp").astype(BF16)
    send_prod = (
        jnp.dot(route_map, product_bf, preferred_element_type=F32)
        .astype(BF16)
        .reshape(experts, capacity, model_width)
    )
    received = exchange(send_prod)
    grad_hidden = contract_last(received.reshape(slot_total, model_width), weight_down)
    grad_gate = (grad_hidden * gate_coef).astype(BF16)
    grad_up = (grad_hidden * up_coef).astype(BF16)
    vjp_part = contract_last(grad_gate, weight_gate) + contract_last(grad_up, weight_up)
    returned_two = exchange(vjp_part.astype(BF16).reshape(experts, capacity, model_width))
    result_part = jnp.dot(
        combine_map,
        returned_two.reshape(slot_total, -1).astype(F32),
        precision=lax.Precision.HIGHEST,
        preferred_element_type=F32,
    )
    result = lax.psum_scatter(result_part, "dp", scatter_dimension=0, tiled=True)
    probe_f = tangent[0].astype(F32)
    probe_result, result_sq, probe_sq = lax.psum(
        (jnp.sum(probe_f * result), jnp.sum(result * result), jnp.sum(probe_f * probe_f)),
        ("dp", "expert"),
    )
    total_cells = lax.axis_size("dp") * lax.axis_size("expert") * tok_dev * model_width
    next_tangent = (result * lax.rsqrt(result_sq / total_cells + 1e-06)).astype(BF16)
    lipschitz = jnp.sqrt(probe_result / probe_sq)
    return (next_tangent[None], lipschitz)


def solution(mesh):
    return jax.shard_map(
        body,
        mesh=mesh,
        in_specs=(
            P("expert", "dp", None),
            P("expert", "dp", None),
            P("expert", "dp", None),
            P("expert", "dp", None),
            P("expert", None, "dp"),
            P("expert", None, "dp"),
            P("expert", "dp", None),
        ),
        out_specs=(P("expert", "dp", None), P()),
        check_vma=False,
    )
```

profile of v0, /device:TPU:1, one launch (start us, length us, event | category | flops | bytes accessed | tf_op | source)
XLA Modules:
  0.0 496.2 jit_solution(14524132102642386330)
XLA Ops:
  7.2 0.7 fusion.50
  7.9 0.7 convert_bitcast_fusion.1
  8.6 0.9 concatenate.6
  9.4 23.7 %all-gather = bf16[8,2,14464]{2,1,0:T(2,128)(2,1)S(1)} all-gather(bf16[1,2,14464]{2,1,0:T(2,128)(2,1)S(1)} %bitcast.125), channel_id=1, replica_groups=mesh['dp'=8,'expert'=32] {'dp'}, dimensions={0}, use_global_device_ids=true | all-gather | bytes 520704 | tf_op jit(solution)/shard_map/all_gather | solution.py:41
  33.1 0.2 reshape.97
  33.3 0.1 eq.39
  33.4 0.1 fusion.43
  33.5 0.2 reduce_window_sum.11
  33.7 0.2 select_reduce_fusion.1
  33.9 0.1 reduce_sum.57
  34.0 0.1 convert_reduce_fusion
  34.1 0.1 copy.10
  34.2 0.2 multiply_convert_fusion
  34.5 0.1 convert_element_type.99
  34.6 2.0 convolution_convert_fusion
  36.7 0.0 copy-start.2
  36.7 98.5 %all_to_all.20 = bf16[32,16,7168]{2,1,0:T(8,128)(2,1)S(1)} all-to-all(bf16[32,16,7168]{2,1,0:T(8,128)(2,1)S(1)} %bitcast.123), channel_id=1, replica_groups=mesh['dp'=8,'expert'=32] {'expert'}, dimensions={0} | all-to-all | bytes 14680064 | tf_op jit(solution)/shard_map/all_to_all | solution.py:20
  135.1 0.0 copy-done.2
  135.2 2.1 fusion.6
  137.2 0.0 copy-done.4
  137.2 0.0 copy-start
  137.2 2.1 fusion.4
  139.3 0.0 copy-done
  139.3 3.1 fusion.1
  142.4 4.8 all-to-all-start.1
  147.2 0.0 all-reduce.5.cloned.1.call-start
  147.2 0.1 fusion.48
  147.3 0.1 select_reduce_fusion
  147.4 44.9 %all-to-all-done.1 = bf16[32,8,7168]{2,1,0:T(8,128)(2,1)} async-done(((bf16[32,8,7168]{2,1,0:T(8,128)(2,1)}), bf16[32,8,7168]{2,1,0:T(8,128)(2,1)}, u32[]{:S(2)}, u32[]{:S(2)}) %all-to-all-start.1) | async-done | bytes 3670048 | tf_op jit(solution)/shard_map/all_to_all | solution.py:20
  192.3 3.6 fusion.14
  195.9 28.2 %all-reduce.6 = bf16[16,7168]{1,0:T(8,128)(2,1)S(1)} all-reduce(f32[16,7168]{1,0:T(8,128)S(1)} %fusion.14), channel_id=1, replica_groups=mesh['dp'=8,'expert'=32] {'dp'}, use_global_device_ids=true, to_apply=%region_4.5 | all-reduce | flops 114688 | bytes 688128 | tf_op jit(solution)/shard_map/psum | solution.py:106
  224.1 1.1 fusion.2
  225.3 0.0 copy-start.1
  225.3 57.6 %all_to_all.21 = bf16[32,8,7168]{2,1,0:T(8,128)(2,1)S(1)} all-to-all(bf16[32,8,7168]{2,1,0:T(8,128)(2,1)S(1)} %fusion.2), channel_id=1, replica_groups=mesh['dp'=8,'expert'=32] {'expert'}, dimensions={0} | all-to-all | bytes 7340032 | tf_op jit(solution)/shard_map/all_to_all | solution.py:20
  282.9 1.1 fusion.12
  284.0 0.9 copy-done.3
  284.9 1.2 fusion.19
  286.1 0.8 copy-done.5
  287.0 1.2 fusion.3
  288.1 48.9 %all_to_all.22 = bf16[32,8,7168]{2,1,0:T(8,128)(2,1)S(1)} all-to-all(bf16[32,8,7168]{2,1,0:T(8,128)(2,1)S(1)} %fusion.3), channel_id=1, replica_groups=mesh['dp'=8,'expert'=32] {'expert'}, dimensions={0} | all-to-all | bytes 7340032 | tf_op jit(solution)/shard_map/all_to_all | solution.py:20
  337.0 2.3 fusion.10
  339.4 0.0 all-reduce.5.cloned.1.call-update
  339.4 0.6 dynamic-slice
  340.6 62.1 %all-reduce.5.cloned.1.call-done = f32[16,7168]{1,0:T(8,128)} async-done(((f32[16,7168]{1,0:T(8,128)}), f32[16,7168]{1,0:T(8,128)}) %all-reduce.5.cloned.1.call-update) | async-done | bytes 458768
  402.8 0.0 copy-done.6
  402.8 1.7 fusion.44
  404.5 80.1 %all-reduce.1 = (f32[]{:T(128)}, f32[]{:T(128)}, f32[]{:T(128)}) all-reduce(f32[]{:T(128)} %get-tuple-element.3, f32[]{:T(128)} %get-tuple-element.2, f32[]{:T(128)} %get-tuple-element.4), channel_id=1, replica_groups=mesh['dp'=8,'expert'=32] {'dp','expert'}, use_global_device_ids=true, to_apply=%region_7.8 | all-reduce | flops 3 | bytes 24 | tf_op jit(solution)/shard_map/psum | solution.py:126
  486.6 1.6 fusion.46
  (13 shorter events, 0.1 us)
Async XLA Ops:
  36.7 98.5 %copy-start.2 = (bf16[1,7168,256]{2,1,0:T(8,128)(2,1)S(1)}, bf16[1,7168,256]{2,1,0:T(8,128)(2,1)}, u32[]{:S(2)}) copy-start(bf16[1,7168,256]{2,1,0:T(8,128)(2,1)} %param.11) | copy-start | bytes 11010052
  135.2 2.1 copy-start.4
  137.2 2.1 copy-start
  142.4 50.0 %all-to-all-start.1 = ((bf16[32,8,7168]{2,1,0:T(8,128)(2,1)}), bf16[32,8,7168]{2,1,0:T(8,128)(2,1)}, u32[]{:S(2)}, u32[]{:S(2)}) async-start(bf16[32,8,7168]{2,1,0:T(8,128)(2,1)} %fusion.1), calls=%async_computation.1 | async-start | bytes 7340032 | tf_op jit(solution)/shard_map/all_to_all | solution.py:20
  147.2 255.6 %all-reduce.5.cloned.1.call-start = ((), (), s32[]{:S(2)}) async-start(), calls=%async_computation.4 | async-start | bytes 917504
  225.3 57.6 %copy-start.1 = (bf16[1,256,7168]{2,1,0:T(8,128)(2,1)S(1)}, bf16[1,256,7168]{2,1,0:T(8,128)(2,1)}, u32[]{:S(2)}) copy-start(bf16[1,256,7168]{2,1,0:T(8,128)(2,1)} %param.13) | copy-start | bytes 11010052
  282.9 2.0 copy-start.3
  284.9 2.0 copy-start.5
  337.0 2.4 copy-start.7
  337.0 65.7 %copy-start.6 = (bf16[1,2,7168]{2,1,0:T(2,128)(2,1)S(1)}, bf16[1,2,7168]{2,1,0:T(2,128)(2,1)}, u32[]{:S(2)}) copy-start(bf16[1,2,7168]{2,1,0:T(2,128)(2,1)} %param.8) | copy-start | bytes 86020
Sparse Core Ops, SparseCore 0:
  339.5 63.2 all-reduce.4
where the time goes:
time: 497 us; the launch traced here: 496 us
  blocking collectives  337 us (68%)
  waiting for transfers between devices  107 us (22%)
  matrix products  19.7 us (4%)
  between operations  18.1 us (4%)
  other arithmetic  5.68 us (1%)
    all_to_all x3, blocking collectives, exchange(): lax.all_to_all(value, 'expert', split_axis=0, concat_axis=0, tiled=True)  205 us
    psum x1, blocking collectives, body(): lax.psum((jnp.sum(probe_f * result), jnp.sum(result * result), jnp.sum(pr...  80.1 us
    unnamed x2, waiting for transfers between devices  62.1 us
    all_to_all x1, waiting for transfers between devices, exchange(): lax.all_to_all(value, 'expert', split_axis=0, concat_axis=0, tiled=True)  44.9 us
    psum x1, blocking collectives, body(): product_bf = lax.psum(product_part, 'dp').astype(BF16)  28.2 us
    all_gather x1, blocking collectives, body(): col = lax.all_gather(packed, 'dp', axis=0, tiled=True)  23.7 us
  transfers between devices with their start and end apart: 2, of which 2 were waited for; matrix products, arithmetic and copies ran while one was open for 0% of the time, Pallas kernels for 0%

commit v1 on v0

--- a/solution.py
+++ b/solution.py
@@ -38,7 +38,9 @@
     if pad:
         pieces.append(jnp.zeros((tok_dev, pad), BF16))
     packed = jnp.concatenate(pieces, axis=1)
-    col = lax.all_gather(packed, "dp", axis=0, tiled=True)
+    col = jnp.concatenate(
+        lax.all_to_all(jnp.stack([packed] * lax.axis_size("dp")), "dp", 0, 0), axis=0
+    )
     col_count = col.shape[0]
     meta = col[:, 2 * model_width : width].astype(jnp.int32)
     col_ids = meta[:, :top_count]

time: 497 us -> 492 us (0.990)
  blocking collectives: 337 us -> 306 us
  waiting for transfers between devices: 107 us -> 123 us
  starting transfers between devices: 4.86 us -> 13.9 us
    all_gather x1 -> x0, blocking collectives: 23.7 us -> none  [body(): col = lax.all_gather(packed, 'dp', axis=0, tiled=True)]
    all_to_all x0 -> x1, waiting for transfers between devices: none -> 16.6 us  [body(): lax.all_to_all(jnp.stack([packed] * lax.axis_size('dp')), 'dp', 0, 0)]
    all_to_all x0 -> x1, starting transfers between devices: none -> 9 us  [body(): lax.all_to_all(jnp.stack([packed] * lax.axis_size('dp')), 'dp', 0, 0)]
    all_to_all x3, blocking collectives: 205 us -> 200 us  [exchange(): lax.all_to_all(value, 'expert', split_axis=0, concat_axis=0, tiled=True)]
  transfers between devices with their start and end apart: 2 -> 3, of which waited for: 2 -> 3; matrix products, arithmetic and copies ran while one was open for 0% -> 0% of each run, Pallas kernels for 0% -> 0%
where the time goes in v1:
time: 492 us; the launch traced here: 491 us
  blocking collectives  306 us (62%)
  waiting for transfers between devices  123 us (25%)
  matrix products  19.7 us (4%)
  between operations  18.1 us (4%)
  starting transfers between devices  13.9 us (3%)
  other arithmetic  5.68 us (1%)
    all_to_all x3, blocking collectives, exchange(): lax.all_to_all(value, 'expert', split_axis=0, concat_axis=0, tiled=True)  200 us
    psum x1, blocking collectives, body(): lax.psum((jnp.sum(probe_f * result), jnp.sum(result * result), jnp.sum(pr...  80.1 us
    unnamed x2, waiting for transfers between devices  61.3 us
    all_to_all x1, waiting for transfers between devices, exchange(): lax.all_to_all(value, 'expert', split_axis=0, concat_axis=0, tiled=True)  44.9 us
    psum x1, blocking collectives, body(): product_bf = lax.psum(product_part, 'dp').astype(BF16)  26.2 us
    all_to_all x1, waiting for transfers between devices, body(): lax.all_to_all(jnp.stack([packed] * lax.axis_size('dp')), 'dp', 0, 0)  16.6 us
  transfers between devices with their start and end apart: 3, of which 3 were waited for; matrix products, arithmetic and copies ran while one was open for 0% of the time, Pallas kernels for 0%

profile of v1, /device:TPU:1, one launch (start us, length us, event | category | flops | bytes accessed | tf_op | source)
XLA Modules:
  0.0 490.8 jit_solution(16833712536492034778)
XLA Ops:
  7.2 0.7 fusion.50
  7.9 0.7 convert_bitcast_fusion.1
  8.5 0.9 concatenate.6
  9.4 1.0 stack.2
  10.4 9.0 %all-to-all-start = ((bf16[8,2,14464]{2,1,0:T(2,128)(2,1)}), bf16[8,2,14464]{2,1,0:T(2,128)(2,1)S(1)}, u32[]{:S(2)}, u32[]{:S(2)}) async-start(bf16[8,2,14464]{2,1,0:T(2,128)(2,1)} %stack.2), calls=%async_computation | async-start | bytes 925696 | tf_op jit(solution)/shard_map/all_to_all | solution.py:42
  19.5 16.6 %all-to-all-done = bf16[8,2,14464]{2,1,0:T(2,128)(2,1)S(1)} async-done(((bf16[8,2,14464]{2,1,0:T(2,128)(2,1)}), bf16[8,2,14464]{2,1,0:T(2,128)(2,1)S(1)}, u32[]{:S(2)}, u32[]{:S(2)}) %all-to-all-start) | async-done | bytes 462880 | tf_op jit(solution)/shard_map/all_to_all | solution.py:42
  36.0 0.2 reshape.94
  36.2 0.1 eq.39
  36.3 0.1 fusion.43
  36.4 0.2 reduce_window_sum.11
  36.6 0.2 select_reduce_fusion.1
  36.8 0.1 reduce_sum.57
  36.9 0.1 convert_reduce_fusion
  37.0 0.1 copy.10
  37.1 0.2 multiply_convert_fusion
  37.4 0.1 convert_element_type.99
  37.5 2.0 convolution_convert_fusion
  39.6 0.0 copy-start.2
  39.6 92.2 %all_to_all.25 = bf16[32,16,7168]{2,1,0:T(8,128)(2,1)S(1)} all-to-all(bf16[32,16,7168]{2,1,0:T(8,128)(2,1)S(1)} %bitcast.122), channel_id=1, replica_groups=mesh['dp'=8,'expert'=32] {'expert'}, dimensions={0} | all-to-all | bytes 14680064 | tf_op jit(solution)/shard_map/all_to_all | solution.py:20
  131.8 2.1 fusion.6
  133.8 0.0 copy-start
  133.9 2.1 fusion.4
  135.9 0.0 copy-done
  135.9 3.1 fusion.1
  139.0 4.8 all-to-all-start.2
  143.8 0.0 all-reduce.5.cloned.1.call-start
  143.9 0.1 fusion.48
  143.9 0.1 select_reduce_fusion
  144.1 44.9 %all-to-all-done.2 = bf16[32,8,7168]{2,1,0:T(8,128)(2,1)} async-done(((bf16[32,8,7168]{2,1,0:T(8,128)(2,1)}), bf16[32,8,7168]{2,1,0:T(8,128)(2,1)}, u32[]{:S(2)}, u32[]{:S(2)}) %all-to-all-start.2) | async-done | bytes 3670048 | tf_op jit(solution)/shard_map/all_to_all | solution.py:20
  189.0 3.6 fusion.14
  192.5 26.2 %all-reduce.6 = bf16[16,7168]{1,0:T(8,128)(2,1)S(1)} all-reduce(f32[16,7168]{1,0:T(8,128)S(1)} %fusion.14), channel_id=1, replica_groups=mesh['dp'=8,'expert'=32] {'dp'}, use_global_device_ids=true, to_apply=%region_4.5 | all-reduce | flops 114688 | bytes 688128 | tf_op jit(solution)/shard_map/psum | solution.py:108
  218.7 1.1 fusion.2
  219.9 0.0 copy-start.1
  219.9 58.5 %all_to_all.26 = bf16[32,8,7168]{2,1,0:T(8,128)(2,1)S(1)} all-to-all(bf16[32,8,7168]{2,1,0:T(8,128)(2,1)S(1)} %fusion.2), channel_id=1, replica_groups=mesh['dp'=8,'expert'=32] {'expert'}, dimensions={0} | all-to-all | bytes 7340032 | tf_op jit(solution)/shard_map/all_to_all | solution.py:20
  278.4 1.1 fusion.12
  279.5 0.9 copy-done.3
  280.4 1.2 fusion.19
  281.6 0.8 copy-done.5
  282.4 1.2 fusion.3
  283.6 48.9 %all_to_all.27 = bf16[32,8,7168]{2,1,0:T(8,128)(2,1)S(1)} all-to-all(bf16[32,8,7168]{2,1,0:T(8,128)(2,1)S(1)} %fusion.3), channel_id=1, replica_groups=mesh['dp'=8,'expert'=32] {'expert'}, dimensions={0} | all-to-all | bytes 7340032 | tf_op jit(solution)/shard_map/all_to_all | solution.py:20
  332.5 2.3 fusion.10
  334.8 0.0 all-reduce.5.cloned.1.call-update
  334.9 0.6 dynamic-slice
  336.1 61.2 %all-reduce.5.cloned.1.call-done = f32[16,7168]{1,0:T(8,128)} async-done(((f32[16,7168]{1,0:T(8,128)}), f32[16,7168]{1,0:T(8,128)}) %all-reduce.5.cloned.1.call-update) | async-done | bytes 458768
  397.4 0.0 copy-done.6
  397.4 1.7 fusion.44
  399.1 80.1 %all-reduce.1 = (f32[]{:T(128)}, f32[]{:T(128)}, f32[]{:T(128)}) all-reduce(f32[]{:T(128)} %get-tuple-element.3, f32[]{:T(128)} %get-tuple-element.2, f32[]{:T(128)} %get-tuple-element.4), channel_id=1, replica_groups=mesh['dp'=8,'expert'=32] {'dp','expert'}, use_global_device_ids=true, to_apply=%region_7.8 | all-reduce | flops 3 | bytes 24 | tf_op jit(solution)/shard_map/psum | solution.py:128
  481.2 1.6 fusion.46
  (15 shorter events, 0.1 us)
Async XLA Ops:
  10.4 25.6 %all-to-all-start = ((bf16[8,2,14464]{2,1,0:T(2,128)(2,1)}), bf16[8,2,14464]{2,1,0:T(2,128)(2,1)S(1)}, u32[]{:S(2)}, u32[]{:S(2)}) async-start(bf16[8,2,14464]{2,1,0:T(2,128)(2,1)} %stack.2), calls=%async_computation | async-start | bytes 925696 | tf_op jit(solution)/shard_map/all_to_all | solution.py:42
  39.6 92.2 %copy-start.2 = (bf16[1,7168,256]{2,1,0:T(8,128)(2,1)S(1)}, bf16[1,7168,256]{2,1,0:T(8,128)(2,1)}, u32[]{:S(2)}) copy-start(bf16[1,7168,256]{2,1,0:T(8,128)(2,1)} %param.11) | copy-start | bytes 11010052
  131.8 2.1 copy-start.4
  133.8 2.1 copy-start
  139.0 50.0 %all-to-all-start.2 = ((bf16[32,8,7168]{2,1,0:T(8,128)(2,1)}), bf16[32,8,7168]{2,1,0:T(8,128)(2,1)}, u32[]{:S(2)}, u32[]{:S(2)}) async-start(bf16[32,8,7168]{2,1,0:T(8,128)(2,1)} %fusion.1), calls=%async_computation.2 | async-start | bytes 7340032 | tf_op jit(solution)/shard_map/all_to_all | solution.py:20
  143.8 253.6 %all-reduce.5.cloned.1.call-start = ((), (), s32[]{:S(2)}) async-start(), calls=%async_computation.5 | async-start | bytes 917504
  219.9 58.5 %copy-start.1 = (bf16[1,256,7168]{2,1,0:T(8,128)(2,1)S(1)}, bf16[1,256,7168]{2,1,0:T(8,128)(2,1)}, u32[]{:S(2)}) copy-start(bf16[1,256,7168]{2,1,0:T(8,128)(2,1)} %param.13) | copy-start | bytes 11010052
  278.4 2.0 copy-start.3
  280.4 2.0 copy-start.5
  332.5 2.4 copy-start.7
  332.5 64.8 %copy-start.6 = (bf16[1,2,7168]{2,1,0:T(2,128)(2,1)S(1)}, bf16[1,2,7168]{2,1,0:T(2,128)(2,1)}, u32[]{:S(2)}) copy-start(bf16[1,2,7168]{2,1,0:T(2,128)(2,1)} %param.8) | copy-start | bytes 86020
Sparse Core Ops, SparseCore 0:
  335.0 62.3 all-reduce.4
